TPU v7x, 512 devices: a whole 4x8x8 slice. The times are simulated.
512 devices in a mesh: tm: 64 (over y, x, core), head: 8 (over z).
Axes of the slice: x: 4, y: 8, z: 8, core: 2. Of those that a mesh axis runs over, the one named last changes fastest.
Arguments:
- queries: bfloat16 [24576, 5120], P('tm', 'head')
- keys: bfloat16 [24576, 5120], P('tm', 'head')
- values: bfloat16 [24576, 5120], P('tm', 'head')
- text_keys: bfloat16 [512, 5120], P('tm', 'head'), may hold values from -6 to 6
- text_values: bfloat16 [512, 5120], P('tm', 'head')
- out_weight: bfloat16 [5120, 5120], P('head', 'tm'), may hold values from -0.25 to 0.25
- windows: int32 [64], replicated, may hold values from 0 to 4, as said below
- lengths: int32 [64], replicated, may hold values from 96 to 384, as said below
Outputs:
- mixed: bfloat16 [24576, 5120], P('tm', 'head')
Inputs may be any that keep to these rules, and one draw needn't show every extreme that they name: windows reach 4 for some frame in every draw. `lengths`: some frame is full in every draw.
All inputs are finite; a program needn't handle non-finite values.
Results may differ from a plain program's by a relative error of at most 0.014.
Values may be sent and summed in bfloat16 or wider, within the bound.
No kernel may reach another device: no remote copies, remote signals or barrier semaphores. Data moves between devices by JAX's collectives and lax.ppermute only.
A program may use at most 64 MiB of HBM per device.

v0:
```python
import math
import jax
import jax.numpy as jnp
from jax import lax
from jax.sharding import PartitionSpec as P

HD = 128
WIN = 4
FRAME_AXES = ("y", "x", "c")
CHIP_AXES = ("y", "x")
GATHER_SPARE = 8


def shift_frames(value, steps):
    count = lax.axis_size(FRAME_AXES)
    return lax.ppermute(
        value, FRAME_AXES, [(source, source + steps) for source in range(count - steps)]
    )


def relay_back(value, chips_back):
    ys, xs, cs = (lax.axis_size(name) for name in FRAME_AXES)
    count = ys * xs * cs
    first, second = ([], [])
    for y in range(ys):
        for x in range(xs):
            for c in range(cs):
                source = (y * xs + x) * cs + c
                middle = (y * xs + (x - 1) % xs) * cs + c
                first.append((source, middle))
                target = source + chips_back * cs
                if target < count:
                    second.append((middle, target))
    hop = lax.ppermute(value, FRAME_AXES, first)
    return lax.ppermute(hop, FRAME_AXES, second)


def swap_cores(value):
    return lax.ppermute(value, "c", [(0, 1), (1, 0)])


def on_device(queries, keys, values, text_keys, text_values, out_weight, windows, lengths):
    rows = queries.shape[0]
    width = queries.shape[1]
    local_heads = width // HD
    groups = lax.axis_size("head")
    scale = 1.0 / math.sqrt(HD)
    position = lax.axis_index(FRAME_AXES)
    core = lax.axis_index("c")
    first_core = core == 0
    chips = lax.axis_size(CHIP_AXES)
    block = out_weight.shape[1]
    tokens = text_keys.shape[0]
    spare = jnp.zeros((width, GATHER_SPARE), out_weight.dtype)
    packed = jnp.concatenate([out_weight, text_keys.T, text_values.T, spare], axis=1)
    packed, keys, values = lax.optimization_barrier((packed, keys, values))
    packed = lax.all_gather(
        lax.all_gather(packed, "y", axis=1, tiled=True), "x", axis=1, tiled=True
    )
    own = jnp.stack([keys, values])
    back2 = shift_frames(own, 2)
    back4 = relay_back(own, 2)
    back1 = swap_cores(jnp.where(first_core, own, back2))
    back3 = swap_cores(jnp.where(first_core, back2, back4))
    kv_list = [own, back1, back2, back3, back4]
    token_ids = jnp.arange(rows, dtype=jnp.int32)
    own_window = windows[position]
    mask_list = []
    for step in range(WIN + 1):
        source = position - step
        usable = (step <= own_window) & (source >= 0)
        source_len = lengths[jnp.maximum(source, 0)]
        mask_list.append(usable & (token_ids < source_len))
    key_mask = jnp.concatenate(mask_list)
    all_keys = jnp.concatenate([p[0] for p in kv_list], axis=0)
    all_values = jnp.concatenate([p[1] for p in kv_list], axis=0)
    frame_parts = []
    for head_index in range(local_heads):
        lower = head_index * HD
        query_h = queries[:, lower : lower + HD]
        scores = (
            lax.dot_general(
                query_h,
                all_keys[:, lower : lower + HD],
                (((1,), (1,)), ((), ())),
                preferred_element_type=jnp.float32,
            )
            * scale
        )
        scores = jnp.where(key_mask[None, :], scores, -jnp.inf)
        top_f = jnp.max(scores, axis=-1, keepdims=True)
        weights = jnp.exp(scores - top_f)
        total_f = jnp.sum(weights, axis=-1, keepdims=True)
        acc_f = jnp.dot(
            weights.astype(jnp.bfloat16),
            all_values[:, lower : lower + HD],
            preferred_element_type=jnp.float32,
        )
        frame_parts.append((top_f, total_f, acc_f))
    packed, frame_parts = lax.optimization_barrier((packed, frame_parts))
    packed = packed.reshape(width, chips, -1)
    text_own = packed[:, :, block : block + 2 * tokens]
    text_pair = jnp.stack([text_own, swap_cores(text_own)])
    text_kt = text_pair[:, :, :, :tokens].transpose(1, 0, 2, 3).reshape(width, -1)
    text_vt = text_pair[:, :, :, tokens:].transpose(1, 0, 2, 3).reshape(width, -1)
    weight_own = packed[:, :, :block]
    weight_other = swap_cores(weight_own)
    weight_pair = jnp.where(
        first_core, jnp.stack([weight_own, weight_other]), jnp.stack([weight_other, weight_own])
    )
    head_outputs = []
    for head_index in range(local_heads):
        lower = head_index * HD
        query_h = queries[:, lower : lower + HD]
        top_f, total_f, acc_f = frame_parts[head_index]
        scores_t = (
            jnp.dot(query_h, text_kt[lower : lower + HD], preferred_element_type=jnp.float32)
            * scale
        )
        top_t = jnp.max(scores_t, axis=-1, keepdims=True)
        weights_t = jnp.exp(scores_t - top_t)
        total_t = jnp.sum(weights_t, axis=-1, keepdims=True)
        acc_t = lax.dot_general(
            weights_t.astype(jnp.bfloat16),
            text_vt[lower : lower + HD],
            (((1,), (1,)), ((), ())),
            preferred_element_type=jnp.float32,
        )
        top = jnp.maximum(top_f, top_t)
        keep_f = jnp.exp(top_f - top)
        keep_t = jnp.exp(top_t - top)
        attended = (acc_f * keep_f + acc_t * keep_t) / (total_f * keep_f + total_t * keep_t)
        head_outputs.append(attended.astype(jnp.bfloat16))
    attended_all = jnp.concatenate(head_outputs, axis=1)
    ys = lax.axis_size("y")
    xs = lax.axis_size("x")
    w5 = weight_pair.reshape(2, width, xs, ys, block)
    partial_out = jnp.einsum(
        "rk,ckxyn->yrcxn", attended_all, w5, preferred_element_type=jnp.float32
    )
    partial_out = partial_out.reshape(groups, rows, -1)
    mixed = lax.psum_scatter(
        partial_out.astype(jnp.bfloat16), "head", scatter_dimension=0, tiled=True
    )
    mixed = mixed.reshape(rows, 2, xs, block)
    return mixed.transpose(0, 2, 1, 3).reshape(rows, -1)


def solution(mesh):
    frames, heads = mesh.devices.shape
    cores = 2
    xs = 4 if frames % (4 * cores) == 0 else 1
    grid = mesh.devices.reshape(frames // (xs * cores), xs, cores, heads)
    fine = jax.sharding.Mesh(grid, FRAME_AXES + ("head",))
    return jax.shard_map(
        on_device,
        mesh=fine,
        in_specs=(
            P(FRAME_AXES, "head"),
            P(FRAME_AXES, "head"),
            P(FRAME_AXES, "head"),
            P(FRAME_AXES, "head"),
            P(FRAME_AXES, "head"),
            P("head", FRAME_AXES),
            P(),
            P(),
        ),
        out_specs=P(FRAME_AXES, "head"),
        check_vma=False,
    )
```

profile of v0, /device:TPU:1, one launch (start us, length us, event | category | flops | bytes accessed | tf_op | source)
XLA Modules:
  0.0 202.4 jit_solution(5313471305251070740)
XLA Ops:
  6.6 1.7 maximum_maximum_fusion
  8.4 2.3 %pad_maximum_fusion = bf16[2,384,640]{2,1,0:T(8,128)(2,1)} fusion(bf16[1,384,640]{2,1,0:T(8,128)(2,1)} %bitcast.91, bf16[1,384,640]{2,1,0:T(8,128)(2,1)} %bitcast.89), kind=kLoop, calls=%fused_computation.76 | loop fusion | flops 491520 | bytes 1966080 | tf_op jit(solution)/shard_map/stack | solution.py:60
  10.6 5.2 %collective-permute-start.2 = (bf16[2,384,640]{2,1,0:T(8,128)(2,1)}, bf16[2,384,640]{2,1,0:T(8,128)(2,1)}, u32[]{:S(2)}, u32[]{:S(2)}) collective-permute-start(bf16[2,384,640]{2,1,0:T(8,128)(2,1)} %pad_maximum_fusion), channel_id=1, source_target_pairs={{0,48},{8,56},{16,0},{24,8},{32,16},{40,24},{48,32},{56,40},{64,11... | collective-permute-start | bytes 2949128 | tf_op jit(solution)/shard_map/ppermute | solution.py:34
  15.9 1.4 collective-permute-start
  17.3 16.6 %collective-permute-done.2 = bf16[2,384,640]{2,1,0:T(8,128)(2,1)} collective-permute-done((bf16[2,384,640]{2,1,0:T(8,128)(2,1)}, bf16[2,384,640]{2,1,0:T(8,128)(2,1)}, u32[]{:S(2)}, u32[]{:S(2)}) %collective-permute-start.2) | collective-permute-done | bytes 983072 | tf_op jit(solution)/shard_map/ppermute | solution.py:34
  33.9 5.4 %collective-permute-start.3 = (bf16[2,384,640]{2,1,0:T(8,128)(2,1)}, bf16[2,384,640]{2,1,0:T(8,128)(2,1)S(1)}, u32[]{:S(2)}, u32[]{:S(2)}) collective-permute-start(bf16[2,384,640]{2,1,0:T(8,128)(2,1)} %collective-permute-done.2), channel_id=1, source_target_pairs={{48,32},{56,40},{0,48},{8,56},{16,64},{24,72},{32,80},{40,88},{112... | collective-permute-start | bytes 2949128 | tf_op jit(solution)/shard_map/ppermute | solution.py:35
  39.3 16.6 %all-gather.3.cloned.1.call-done = bf16[640,832]{0,1:T(8,128)(2,1)} async-done(((bf16[640,104]{0,1:T(8,128)(2,1)}), bf16[640,832]{0,1:T(8,128)(2,1)}) %all-gather.3.cloned.1.call-update) | async-done | bytes 1064976 | tf_op jit(solution)/shard_map/all_gather | solution.py:58
  56.3 1.5 broadcast_select_fusion
  57.9 7.0 %collective-permute-start.1 = (bf16[2,384,640]{2,1,0:T(8,128)(2,1)}, bf16[2,384,640]{2,1,0:T(8,128)(2,1)}, u32[]{:S(2)}, u32[]{:S(2)}) collective-permute-start(bf16[2,384,640]{2,1,0:T(8,128)(2,1)} %get-tuple-element.71), channel_id=1, source_target_pairs={{0,8},{8,0},{1,9},{9,1},{2,10},{10,2},{3,11},{11,3},{4,12},{12,4},... | collective-permute-start | bytes 2949128 | tf_op jit(solution)/shard_map/ppermute | solution.py:39
  65.0 0.6 dynamic_slice.18
  68.8 0.7 fusion.137
  69.5 0.6 fusion.109
  70.4 0.7 fusion.110
  71.3 1.9 collective-permute-start.4
  73.3 0.6 fusion.111
  74.1 0.7 fusion.112
  75.1 0.7 fusion.113
  76.1 1.4 fusion.82
  77.7 1.4 fusion.80
  79.3 0.7 fusion.142
  80.0 0.5 fusion.21
  80.6 0.7 fusion.141
  81.3 0.5 fusion.19
  81.8 0.7 fusion.140
  82.5 0.5 fusion.17
  83.1 0.7 fusion.139
  83.8 0.5 fusion.15
  84.3 0.7 fusion.138
  85.0 0.5 fusion.13
  85.5 0.6 fusion.22
  86.2 0.6 fusion.24
  86.8 0.6 fusion.26
  87.4 0.6 fusion.28
  88.0 0.6 fusion.30
  88.6 27.8 %all-gather.5.cloned.1.call-done = bf16[640,3328]{0,1:T(8,128)(2,1)} async-done(((bf16[640,832]{0,1:T(8,128)(2,1)}), bf16[640,3328]{0,1:T(8,128)(2,1)}) %all-gather.5.cloned.1.call-update) | async-done | bytes 4259856 | tf_op jit(solution)/shard_map/all_gather | solution.py:57
  116.4 1.2 slice_bitcast_fusion.8
  117.6 2.6 %collective-permute-start.6 = (bf16[640,32,16]{0,2,1:T(8,128)(2,1)S(1)}, bf16[640,32,16]{0,2,1:T(8,128)(2,1)S(1)}, u32[]{:S(2)}, u32[]{:S(2)}) collective-permute-start(bf16[640,32,16]{0,2,1:T(8,128)(2,1)S(1)} %get-tuple-element.59), channel_id=1, source_target_pairs={{0,8},{8,0},{1,9},{9,1},{2,10},{10,2},{3,11},{11,3},{4,12},{12,4},... | collective-permute-start | bytes 1966088 | tf_op jit(solution)/shard_map/ppermute | solution.py:39
  120.2 2.2 %slice.211 = bf16[640,32,80]{0,2,1:T(8,128)(2,1)S(1)} slice(bf16[640,32,104]{0,2,1:T(8,128)(2,1)} %bitcast.94), slice={[0:640], [0:32], [0:80]} | slice | bytes 6553600 | tf_op jit(solution)/shard_map/slice | solution.py:106
  122.4 2.1 %collective-permute-start.5 = (bf16[640,32,80]{0,2,1:T(8,128)(2,1)S(1)}, bf16[640,32,80]{0,2,1:T(8,128)(2,1)S(1)}, u32[]{:S(2)}, u32[]{:S(2)}) collective-permute-start(bf16[640,32,80]{0,2,1:T(8,128)(2,1)S(1)} %slice.211), channel_id=1, source_target_pairs={{0,8},{8,0},{1,9},{9,1},{2,10},{10,2},{3,11},{11,3},{4,12},{12,4},... | collective-permute-start | bytes 9830408 | tf_op jit(solution)/shard_map/ppermute | solution.py:39
  128.1 0.4 fusion.52
  128.5 0.4 fusion.54
  128.9 0.4 fusion.56
  129.3 0.8 collective-permute-done.5
  130.1 4.7 %convert_bitcast_fusion = bf16[8,384,2,4,80]{1,4,0,3,2:T(8,128)(2,1)S(1)} fusion(bf16[1,640,4,8,80]{1,4,3,2,0:T(8,128)(2,1)S(1)} %bitcast.111, bf16[1,640,4,8,80]{1,4,3,2,0:T(8,128)(2,1)S(1)} %bitcast.95, pred[]{:T(512)S(6)} %eq.3, bf16[384,640]{1,0:T(8,128)(2,1)S(1)} %fusion.56), kind=kOutput, calls=%fused_computation.8 | convolution fusion | flops 2528378880 | bytes 10977281 | tf_op jit(solution)/shard_map/rk,ckxyn->yrcxn/dot_general | solution.py:138
  134.9 2.5 %copy.9 = bf16[8,384,2,4,80]{1,4,3,2,0:T(8,128)(2,1)} copy(bf16[8,384,2,4,80]{1,4,0,3,2:T(8,128)(2,1)S(1)} %convert_bitcast_fusion) | data formatting | bytes 7864320 | tf_op jit(solution)/shard_map/convert_element_type | solution.py:143
  137.4 56.4 %reduce-scatter.2.cloned.1.call-done = bf16[1,384,640]{1,2,0:T(8,128)(2,1)} async-done(((bf16[8,384,640]{1,2,0:T(8,128)(2,1)}), bf16[1,384,640]{1,2,0:T(8,128)(2,1)}) %reduce-scatter.2.cloned.1.call-update) | async-done | bytes 491536 | tf_op jit(solution)/shard_map/reduce_scatter | solution.py:142
  193.8 1.1 copy.10
  194.9 1.0 copy.11
  (62 shorter events, 5.9 us)
Async XLA Ops:
  6.5 49.8 %copy-start.1 = (bf16[384,640]{1,0:T(8,128)(2,1)S(1)}, bf16[384,640]{1,0:T(8,128)(2,1)}, u32[]{:S(2)}) copy-start(bf16[384,640]{1,0:T(8,128)(2,1)} %param.10) | copy-start | bytes 1474564
  6.5 49.8 %copy-start = (bf16[384,640]{1,0:T(8,128)(2,1)S(1)}, bf16[384,640]{1,0:T(8,128)(2,1)}, u32[]{:S(2)}) copy-start(bf16[384,640]{1,0:T(8,128)(2,1)} %param.9) | copy-start | bytes 1474564
  6.5 49.3 %all-gather.3.cloned.1.call-start = ((), (), s32[]{:S(2)}) async-start(), calls=%async_computation.1 | async-start | bytes 1198080 | tf_op jit(solution)/shard_map/all_gather | solution.py:58
  10.6 23.3 %collective-permute-start.2 = (bf16[2,384,640]{2,1,0:T(8,128)(2,1)}, bf16[2,384,640]{2,1,0:T(8,128)(2,1)}, u32[]{:S(2)}, u32[]{:S(2)}) collective-permute-start(bf16[2,384,640]{2,1,0:T(8,128)(2,1)} %pad_maximum_fusion), channel_id=1, source_target_pairs={{0,48},{8,56},{16,0},{24,8},{32,16},{40,24},{48,32},{56,40},{64,11... | collective-permute-start | bytes 2949128 | tf_op jit(solution)/shard_map/ppermute | solution.py:34
  15.9 100.5 %all-gather.5.cloned.1.call-start = ((), (), s32[]{:S(2)}) async-start(), calls=%async_computation.2 | async-start | bytes 5324800 | tf_op jit(solution)/shard_map/all_gather | solution.py:57
  15.9 40.0 %collective-permute-start = (bf16[2,384,640]{2,1,0:T(8,128)(2,1)}, bf16[2,384,640]{2,1,0:T(8,128)(2,1)S(1)}, u32[]{:S(2)}, u32[]{:S(2)}) collective-permute-start(bf16[2,384,640]{2,1,0:T(8,128)(2,1)} %pad_maximum_fusion), channel_id=1, source_target_pairs={{0,16},{8,24},{16,32},{24,40},{32,48},{40,56},{48,64},{56,72},{64,... | collective-permute-start | bytes 2949128 | tf_op jit(solution)/shard_map/ppermute | solution.py:16
  33.9 22.4 %collective-permute-start.3 = (bf16[2,384,640]{2,1,0:T(8,128)(2,1)}, bf16[2,384,640]{2,1,0:T(8,128)(2,1)S(1)}, u32[]{:S(2)}, u32[]{:S(2)}) collective-permute-start(bf16[2,384,640]{2,1,0:T(8,128)(2,1)} %collective-permute-done.2), channel_id=1, source_target_pairs={{48,32},{56,40},{0,48},{8,56},{16,64},{24,72},{32,80},{40,88},{112... | collective-permute-start | bytes 2949128 | tf_op jit(solution)/shard_map/ppermute | solution.py:35
  55.8 9.1 %copy-start.4 = (s32[64]{0:T(128)S(1)}, s32[64]{0:T(128)}, u32[]{:S(2)}) copy-start(s32[64]{0:T(128)} %param.14) | copy-start | bytes 772
  55.8 13.0 %copy-start.3 = (s32[64]{0:T(128)S(1)}, s32[64]{0:T(128)}, u32[]{:S(2)}) copy-start(s32[64]{0:T(128)} %param.15) | copy-start | bytes 772
  55.9 137.9 %reduce-scatter.2.cloned.1.call-start = ((), (), s32[]{:S(2)}) async-start(), calls=%async_computation.3 | async-start | bytes 4423680 | tf_op jit(solution)/shard_map/reduce_scatter | solution.py:142
  57.9 18.2 %collective-permute-start.1 = (bf16[2,384,640]{2,1,0:T(8,128)(2,1)}, bf16[2,384,640]{2,1,0:T(8,128)(2,1)}, u32[]{:S(2)}, u32[]{:S(2)}) collective-permute-start(bf16[2,384,640]{2,1,0:T(8,128)(2,1)} %get-tuple-element.71), channel_id=1, source_target_pairs={{0,8},{8,0},{1,9},{9,1},{2,10},{10,2},{3,11},{11,3},{4,12},{12,4},... | collective-permute-start | bytes 2949128 | tf_op jit(solution)/shard_map/ppermute | solution.py:39
  71.3 6.4 %collective-permute-start.4 = (bf16[2,384,640]{2,1,0:T(8,128)(2,1)}, bf16[2,384,640]{2,1,0:T(8,128)(2,1)}, u32[]{:S(2)}, u32[]{:S(2)}) collective-permute-start(bf16[2,384,640]{2,1,0:T(8,128)(2,1)} %get-tuple-element.70), channel_id=1, source_target_pairs={{0,8},{8,0},{1,9},{9,1},{2,10},{10,2},{3,11},{11,3},{4,12},{12,4},... | collective-permute-start | bytes 2949128 | tf_op jit(solution)/shard_map/ppermute | solution.py:39
  77.5 1.8 copy-start.2
  117.6 6.9 %collective-permute-start.6 = (bf16[640,32,16]{0,2,1:T(8,128)(2,1)S(1)}, bf16[640,32,16]{0,2,1:T(8,128)(2,1)S(1)}, u32[]{:S(2)}, u32[]{:S(2)}) collective-permute-start(bf16[640,32,16]{0,2,1:T(8,128)(2,1)S(1)} %get-tuple-element.59), channel_id=1, source_target_pairs={{0,8},{8,0},{1,9},{9,1},{2,10},{10,2},{3,11},{11,3},{4,12},{12,4},... | collective-permute-start | bytes 1966088 | tf_op jit(solution)/shard_map/ppermute | solution.py:39
  122.4 7.7 %collective-permute-start.5 = (bf16[640,32,80]{0,2,1:T(8,128)(2,1)S(1)}, bf16[640,32,80]{0,2,1:T(8,128)(2,1)S(1)}, u32[]{:S(2)}, u32[]{:S(2)}) collective-permute-start(bf16[640,32,80]{0,2,1:T(8,128)(2,1)S(1)} %slice.211), channel_id=1, source_target_pairs={{0,8},{8,0},{1,9},{9,1},{2,10},{10,2},{3,11},{11,3},{4,12},{12,4},... | collective-permute-start | bytes 9830408 | tf_op jit(solution)/shard_map/ppermute | solution.py:39
Sparse Core Ops, SparseCore 0:
  16.0 39.8 all-gather.2
  57.9 58.4 all-gather.4
  137.5 56.2 reduce-scatter.1
where the time goes:
time: 203 us; the launch traced here: 202 us
  waiting for transfers between devices  119 us (59%)
  starting transfers between devices  25.6 us (13%)
  between operations  16.7 us (8%)
  matrix products  14.7 us (7%)
  local copies, waits for them, and re-layouts  14.2 us (7%)
  other arithmetic  12.5 us (6%)
    reduce_scatter x1, waiting for transfers between devices, on_device(): lax.psum_scatter(partial_out.astype(jnp.bfloat16), 'head', scatter_dimens...  56.4 us
    all_gather x1, waiting for transfers between devices, on_device(): lax.all_gather(lax.all_gather(packed, 'y', axis=1, tiled=True), 'x', axis...  27.8 us
    ppermute x1, waiting for transfers between devices, relay_back(): hop = lax.ppermute(value, FRAME_AXES, first)  16.6 us
    all_gather x1, waiting for transfers between devices, on_device(): lax.all_gather(packed, 'y', axis=1, tiled=True)  16.6 us
    ppermute x4, starting transfers between devices, swap_cores(): return lax.ppermute(value, 'c', [(0, 1), (1, 0)])  13.6 us
    ppermute x1, starting transfers between devices, relay_back(): return lax.ppermute(hop, FRAME_AXES, second)  5.36 us
    ppermute x1, starting transfers between devices, relay_back(): hop = lax.ppermute(value, FRAME_AXES, first)  5.21 us
    dot_general x1, matrix products, on_device(): jnp.einsum('rk,ckxyn->yrcxn', attended_all, w5, preferred_element_type=jn...  4.72 us
  transfers between devices with their start and end apart: 10, of which 6 were waited for; matrix products, arithmetic and copies ran while one was open for 13% of the time, Pallas kernels for 0%

commit v1 on v0

--- a/solution.py
+++ b/solution.py
@@ -54,8 +54,9 @@
     spare = jnp.zeros((width, GATHER_SPARE), out_weight.dtype)
     packed = jnp.concatenate([out_weight, text_keys.T, text_values.T, spare], axis=1)
     packed, keys, values = lax.optimization_barrier((packed, keys, values))
-    packed = lax.all_gather(
-        lax.all_gather(packed, "y", axis=1, tiled=True), "x", axis=1, tiled=True
+    shard_in = lax.all_gather(packed, "y", axis=1, tiled=True)
+    packed = jnp.concatenate(
+        lax.all_to_all(jnp.stack([shard_in for _ in range(lax.axis_size("x"))]), "x", 0, 0), 1
     )
     own = jnp.stack([keys, values])
     back2 = shift_frames(own, 2)

time: 203 us -> 236 us (1.16)
  waiting for transfers between devices: 119 us -> 130 us
  starting transfers between devices: 25.6 us -> 35.6 us
  local copies, waits for them, and re-layouts: 14.2 us -> 22.6 us
    all_gather x2 -> x1, waiting for transfers between devices: 44.4 us -> 3.48 us  [on_device(): shard_in = lax.all_gather(packed, 'y', axis=1, tiled=True)]
    all_to_all x0 -> x1, waiting for transfers between devices: none -> 28.1 us  [on_device(): lax.all_to_all(jnp.stack([shard_in for _ in range(lax.axis_size('x'))]),...]
    ppermute x1, waiting for transfers between devices: 0.39 us -> 17 us  [relay_back(): return lax.ppermute(hop, FRAME_AXES, second)]
    reduce_scatter x1, waiting for transfers between devices: 56.4 us -> 64.2 us  [on_device(): lax.psum_scatter(partial_out.astype(jnp.bfloat16), 'head', scatter_dimens...]
    all_to_all x0 -> x1, starting transfers between devices: none -> 5.41 us  [on_device(): lax.all_to_all(jnp.stack([shard_in for _ in range(lax.axis_size('x'))]),...]
    ppermute x4, starting transfers between devices: 13.6 us -> 18.1 us  [swap_cores(): return lax.ppermute(value, 'c', [(0, 1), (1, 0)])]
    unnamed x18 -> x22, local copies, waits for them, and re-layouts: 4.13 us -> 7.98 us
    another operation x0 -> x1, local copies, waits for them, and re-layouts: none -> 3.52 us  [on_device(): jnp.stack([shard_in for _ in range(lax.axis_size('x'))])]
  transfers between devices with their start and end apart: 10 -> 10, of which waited for: 6 -> 6; matrix products, arithmetic and copies ran while one was open for 13% -> 16% of each run, Pallas kernels for 0% -> 0%
where the time goes in v1:
time: 236 us; the launch traced here: 235 us
  waiting for transfers between devices  130 us (55%)
  starting transfers between devices  35.6 us (15%)
  local copies, waits for them, and re-layouts  22.6 us (10%)
  between operations  17.2 us (7%)
  matrix products  16.4 us (7%)
  other arithmetic  13.3 us (6%)
    reduce_scatter x1, waiting for transfers between devices, on_device(): lax.psum_scatter(partial_out.astype(jnp.bfloat16), 'head', scatter_dimens...  64.2 us
    all_to_all x1, waiting for transfers between devices, on_device(): lax.all_to_all(jnp.stack([shard_in for _ in range(lax.axis_size('x'))]),...  28.1 us
    ppermute x4, starting transfers between devices, swap_cores(): return lax.ppermute(value, 'c', [(0, 1), (1, 0)])  18.1 us
    ppermute x1, waiting for transfers between devices, relay_back(): return lax.ppermute(hop, FRAME_AXES, second)  17 us
    ppermute x1, waiting for transfers between devices, relay_back(): hop = lax.ppermute(value, FRAME_AXES, first)  16.7 us
    unnamed x22, local copies, waits for them, and re-layouts  7.98 us
    all_to_all x1, starting transfers between devices, on_device(): lax.all_to_all(jnp.stack([shard_in for _ in range(lax.axis_size('x'))]),...  5.41 us
    ppermute x1, starting transfers between devices, relay_back(): return lax.ppermute(hop, FRAME_AXES, second)  5.36 us
  transfers between devices with their start and end apart: 10, of which 6 were waited for; matrix products, arithmetic and copies ran while one was open for 16% of the time, Pallas kernels for 0%

profile of v1, /device:TPU:1, one launch (start us, length us, event | category | flops | bytes accessed | tf_op | source)
XLA Modules:
  0.0 235.4 jit_solution(374098044255019366)
XLA Ops:
  6.6 1.7 maximum_maximum_fusion
  8.3 2.2 pad_maximum_fusion
  10.5 5.3 %collective-permute-start.2 = (bf16[2,384,640]{2,1,0:T(8,128)(2,1)}, bf16[2,384,640]{2,1,0:T(8,128)(2,1)}, u32[]{:S(2)}, u32[]{:S(2)}) collective-permute-start(bf16[2,384,640]{2,1,0:T(8,128)(2,1)} %pad_maximum_fusion), channel_id=1, source_target_pairs={{0,48},{8,56},{16,0},{24,8},{32,16},{40,24},{48,32},{56,40},{64,11... | collective-permute-start | bytes 2949128 | tf_op jit(solution)/shard_map/ppermute | solution.py:34
  15.9 1.4 collective-permute-start
  17.3 16.7 %collective-permute-done.2 = bf16[2,384,640]{2,1,0:T(8,128)(2,1)} collective-permute-done((bf16[2,384,640]{2,1,0:T(8,128)(2,1)}, bf16[2,384,640]{2,1,0:T(8,128)(2,1)}, u32[]{:S(2)}, u32[]{:S(2)}) %collective-permute-start.2) | collective-permute-done | bytes 983072 | tf_op jit(solution)/shard_map/ppermute | solution.py:34
  33.9 5.4 %collective-permute-start.3 = (bf16[2,384,640]{2,1,0:T(8,128)(2,1)}, bf16[2,384,640]{2,1,0:T(8,128)(2,1)S(1)}, u32[]{:S(2)}, u32[]{:S(2)}) collective-permute-start(bf16[2,384,640]{2,1,0:T(8,128)(2,1)} %collective-permute-done.2), channel_id=1, source_target_pairs={{48,32},{56,40},{0,48},{8,56},{16,64},{24,72},{32,80},{40,88},{112... | collective-permute-start | bytes 2949128 | tf_op jit(solution)/shard_map/ppermute | solution.py:35
  39.4 17.0 %collective-permute-done.3 = bf16[2,384,640]{2,1,0:T(8,128)(2,1)S(1)} collective-permute-done((bf16[2,384,640]{2,1,0:T(8,128)(2,1)}, bf16[2,384,640]{2,1,0:T(8,128)(2,1)S(1)}, u32[]{:S(2)}, u32[]{:S(2)}) %collective-permute-start.3) | collective-permute-done | bytes 983072 | tf_op jit(solution)/shard_map/ppermute | solution.py:35
  56.4 2.6 %broadcast_select_fusion = (bf16[2,384,640]{2,1,0:T(8,128)(2,1)}, bf16[2,384,640]{2,1,0:T(8,128)(2,1)}) fusion(bf16[2,384,640]{2,1,0:T(8,128)(2,1)S(1)} %collective-permute-done, bf16[2,384,640]{2,1,0:T(8,128)(2,1)S(1)} %collective-permute-done.3, pred[]{:T(512)S(6)} %eq.3, bf16[1,384,640]{2,1,0:T(8,128)(2,1)} %bitcast.95, bf16[1,384,640]{2,1,0:T(8,128)(2,1)} %bitcast.93), kind=kLoop, calls=%fused_computation.77 | loop fusion | flops 1474560 | bytes 4915201 | tf_op jit(solution)/shard_map/jit(_where)/select_n | solution.py:65
  59.0 7.0 %collective-permute-start.1 = (bf16[2,384,640]{2,1,0:T(8,128)(2,1)}, bf16[2,384,640]{2,1,0:T(8,128)(2,1)}, u32[]{:S(2)}, u32[]{:S(2)}) collective-permute-start(bf16[2,384,640]{2,1,0:T(8,128)(2,1)} %get-tuple-element.71), channel_id=1, source_target_pairs={{0,8},{8,0},{1,9},{9,1},{2,10},{10,2},{3,11},{11,3},{4,12},{12,4},... | collective-permute-start | bytes 2949128 | tf_op jit(solution)/shard_map/ppermute | solution.py:39
  66.1 0.7 dynamic_slice.18
  70.3 0.7 fusion.137
  70.9 0.6 fusion.109
  71.8 0.6 fusion.110
  72.7 1.9 collective-permute-start.4
  74.6 0.6 fusion.111
  75.4 0.6 fusion.112
  76.3 0.7 fusion.113
  77.3 1.1 constant_dynamic-update-slice_fusion
  78.3 3.5 %all-gather.2.cloned.1.call-done = bf16[640,832]{0,1:T(8,128)(2,1)} async-done(((bf16[640,104]{0,1:T(8,128)(2,1)}), bf16[640,832]{0,1:T(8,128)(2,1)}) %all-gather.2.cloned.1.call-update) | async-done | bytes 1064976 | tf_op jit(solution)/shard_map/all_gather | solution.py:57
  81.8 3.5 %stack.39 = bf16[4,640,832]{1,2,0:T(8,128)(2,1)} broadcast(bf16[640,832]{0,1:T(8,128)(2,1)} %all-gather.2.cloned.1.call-done), dimensions={1,2} | broadcast | bytes 5324800 | tf_op jit(solution)/shard_map/stack | solution.py:59
  85.3 5.4 %all-to-all-start = ((bf16[4,640,832]{1,2,0:T(8,128)(2,1)}), bf16[4,640,832]{1,2,0:T(8,128)(2,1)}, u32[]{:S(2)}, u32[]{:S(2)}) async-start(bf16[4,640,832]{1,2,0:T(8,128)(2,1)} %stack.39), calls=%async_computation | async-start | bytes 8519680 | tf_op jit(solution)/shard_map/all_to_all | solution.py:59
  90.8 2.2 fusion.82
  93.0 1.0 fusion.81
  94.0 2.2 fusion.80
  96.2 1.1 fusion.79
  97.3 2.4 %fusion.142 = (f32[384]{0:T(512)S(1)}, f32[1920,384]{1,0:T(8,128)S(1)}) fusion(bf16[384,640]{1,0:T(8,128)(2,1)S(1)} %copy-done.4, bf16[1920,640]{1,0:T(8,128)(2,1)} %get-tuple-element.63, pred[1920]{0:T(1024)(128)(4,1)S(1)} %dynamic-update-slice.19), kind=kOutput, calls=%fused_computation.197 | convolution fusion | flops 190955136 | bytes 3542528 | tf_op jit(solution)/shard_map/dot_general | solution.py:83
  99.7 0.7 fusion.141
  101.0 0.5 fusion.19
  101.5 0.7 fusion.140
  102.2 0.5 fusion.17
  102.7 0.7 fusion.139
  104.0 0.7 fusion.138
  105.6 0.6 fusion.22
  106.3 0.6 fusion.24
  106.9 0.6 fusion.26
  107.5 0.6 fusion.28
  108.1 0.6 fusion.30
  108.7 28.1 %all-to-all-done = bf16[4,640,832]{1,2,0:T(8,128)(2,1)} async-done(((bf16[4,640,832]{1,2,0:T(8,128)(2,1)}), bf16[4,640,832]{1,2,0:T(8,128)(2,1)}, u32[]{:S(2)}, u32[]{:S(2)}) %all-to-all-start) | async-done | bytes 4259872 | tf_op jit(solution)/shard_map/all_to_all | solution.py:59
  136.8 1.2 slice_bitcast_fusion.8
  138.0 7.0 %collective-permute-start.6 = (bf16[640,32,16]{0,2,1:T(8,128)(2,1)S(1)}, bf16[640,32,16]{0,2,1:T(8,128)(2,1)S(1)}, u32[]{:S(2)}, u32[]{:S(2)}) collective-permute-start(bf16[640,32,16]{0,2,1:T(8,128)(2,1)S(1)} %get-tuple-element.59), channel_id=1, source_target_pairs={{0,8},{8,0},{1,9},{9,1},{2,10},{10,2},{3,11},{11,3},{4,12},{12,4},... | collective-permute-start | bytes 1966088 | tf_op jit(solution)/shard_map/ppermute | solution.py:39
  145.0 2.2 slice.211
  147.2 2.1 collective-permute-start.5
  154.2 0.8 collective-permute-done.5
  155.0 4.8 %convert_bitcast_fusion = bf16[8,384,2,4,80]{1,4,0,3,2:T(8,128)(2,1)S(1)} fusion(bf16[1,640,4,8,80]{1,4,3,2,0:T(8,128)(2,1)S(1)} %bitcast.112, bf16[1,640,4,8,80]{1,4,3,2,0:T(8,128)(2,1)S(1)} %bitcast.96, pred[]{:T(512)S(6)} %eq.3, bf16[384,640]{1,0:T(8,128)(2,1)S(1)} %fusion.56), kind=kOutput, calls=%fused_computation.8 | convolution fusion | flops 2528378880 | bytes 10977281 | tf_op jit(solution)/shard_map/rk,ckxyn->yrcxn/dot_general | solution.py:139
  159.8 2.5 %copy.9 = bf16[8,384,2,4,80]{1,4,3,2,0:T(8,128)(2,1)} copy(bf16[8,384,2,4,80]{1,4,0,3,2:T(8,128)(2,1)S(1)} %convert_bitcast_fusion) | data formatting | bytes 7864320 | tf_op jit(solution)/shard_map/convert_element_type | solution.py:144
  162.3 64.2 %reduce-scatter.2.cloned.1.call-done = bf16[1,384,640]{1,2,0:T(8,128)(2,1)} async-done(((bf16[8,384,640]{1,2,0:T(8,128)(2,1)}), bf16[1,384,640]{1,2,0:T(8,128)(2,1)}) %reduce-scatter.2.cloned.1.call-update) | async-done | bytes 491536 | tf_op jit(solution)/shard_map/reduce_scatter | solution.py:143
  226.5 1.1 copy.10
  227.6 1.0 copy.11
  (66 shorter events, 8.2 us)
Async XLA Ops:
  6.5 75.3 %all-gather.2.cloned.1.call-start = ((), (), s32[]{:S(2)}) async-start(), calls=%async_computation.2 | async-start | bytes 1198080 | tf_op jit(solution)/shard_map/all_gather | solution.py:57
  10.5 55.6 %copy-start.6 = (s32[64]{0:T(128)S(1)}, s32[64]{0:T(128)}, u32[]{:S(2)}) copy-start(s32[64]{0:T(128)} %param.14) | copy-start | bytes 772
  10.5 59.7 %copy-start.5 = (s32[64]{0:T(128)S(1)}, s32[64]{0:T(128)}, u32[]{:S(2)}) copy-start(s32[64]{0:T(128)} %param.15) | copy-start | bytes 772
  10.5 66.7 %copy-start = (bf16[384,640]{1,0:T(8,128)(2,1)S(1)}, bf16[384,640]{1,0:T(8,128)(2,1)}, u32[]{:S(2)}) copy-start(bf16[384,640]{1,0:T(8,128)(2,1)} %param.9) | copy-start | bytes 1474564
  10.5 66.7 %copy-start.1 = (bf16[384,640]{1,0:T(8,128)(2,1)S(1)}, bf16[384,640]{1,0:T(8,128)(2,1)}, u32[]{:S(2)}) copy-start(bf16[384,640]{1,0:T(8,128)(2,1)} %param.10) | copy-start | bytes 1474564
  10.5 23.4 %collective-permute-start.2 = (bf16[2,384,640]{2,1,0:T(8,128)(2,1)}, bf16[2,384,640]{2,1,0:T(8,128)(2,1)}, u32[]{:S(2)}, u32[]{:S(2)}) collective-permute-start(bf16[2,384,640]{2,1,0:T(8,128)(2,1)} %pad_maximum_fusion), channel_id=1, source_target_pairs={{0,48},{8,56},{16,0},{24,8},{32,16},{40,24},{48,32},{56,40},{64,11... | collective-permute-start | bytes 2949128 | tf_op jit(solution)/shard_map/ppermute | solution.py:34
  15.9 23.4 %collective-permute-start = (bf16[2,384,640]{2,1,0:T(8,128)(2,1)}, bf16[2,384,640]{2,1,0:T(8,128)(2,1)S(1)}, u32[]{:S(2)}, u32[]{:S(2)}) collective-permute-start(bf16[2,384,640]{2,1,0:T(8,128)(2,1)} %pad_maximum_fusion), channel_id=1, source_target_pairs={{0,16},{8,24},{16,32},{24,40},{32,48},{40,56},{48,64},{56,72},{64,... | collective-permute-start | bytes 2949128 | tf_op jit(solution)/shard_map/ppermute | solution.py:16
  33.9 22.4 %collective-permute-start.3 = (bf16[2,384,640]{2,1,0:T(8,128)(2,1)}, bf16[2,384,640]{2,1,0:T(8,128)(2,1)S(1)}, u32[]{:S(2)}, u32[]{:S(2)}) collective-permute-start(bf16[2,384,640]{2,1,0:T(8,128)(2,1)} %collective-permute-done.2), channel_id=1, source_target_pairs={{48,32},{56,40},{0,48},{8,56},{16,64},{24,72},{32,80},{40,88},{112... | collective-permute-start | bytes 2949128 | tf_op jit(solution)/shard_map/ppermute | solution.py:35
  59.0 31.7 %collective-permute-start.1 = (bf16[2,384,640]{2,1,0:T(8,128)(2,1)}, bf16[2,384,640]{2,1,0:T(8,128)(2,1)}, u32[]{:S(2)}, u32[]{:S(2)}) collective-permute-start(bf16[2,384,640]{2,1,0:T(8,128)(2,1)} %get-tuple-element.71), channel_id=1, source_target_pairs={{0,8},{8,0},{1,9},{9,1},{2,10},{10,2},{3,11},{11,3},{4,12},{12,4},... | collective-permute-start | bytes 2949128 | tf_op jit(solution)/shard_map/ppermute | solution.py:39
  72.7 21.3 %collective-permute-start.4 = (bf16[2,384,640]{2,1,0:T(8,128)(2,1)}, bf16[2,384,640]{2,1,0:T(8,128)(2,1)}, u32[]{:S(2)}, u32[]{:S(2)}) collective-permute-start(bf16[2,384,640]{2,1,0:T(8,128)(2,1)} %get-tuple-element.70), channel_id=1, source_target_pairs={{0,8},{8,0},{1,9},{9,1},{2,10},{10,2},{3,11},{11,3},{4,12},{12,4},... | collective-permute-start | bytes 2949128 | tf_op jit(solution)/shard_map/ppermute | solution.py:39
  85.3 51.5 %all-to-all-start = ((bf16[4,640,832]{1,2,0:T(8,128)(2,1)}), bf16[4,640,832]{1,2,0:T(8,128)(2,1)}, u32[]{:S(2)}, u32[]{:S(2)}) async-start(bf16[4,640,832]{1,2,0:T(8,128)(2,1)} %stack.39), calls=%async_computation | async-start | bytes 8519680 | tf_op jit(solution)/shard_map/all_to_all | solution.py:59
  90.7 135.7 %reduce-scatter.2.cloned.1.call-start = ((), (), s32[]{:S(2)}) async-start(), calls=%async_computation.3 | async-start | bytes 4423680 | tf_op jit(solution)/shard_map/reduce_scatter | solution.py:143
  93.0 4.3 %copy-start.4 = (bf16[384,640]{1,0:T(8,128)(2,1)S(1)}, bf16[384,640]{1,0:T(8,128)(2,1)}, u32[]{:S(2)}) copy-start(bf16[384,640]{1,0:T(8,128)(2,1)} %param.8) | copy-start | bytes 1474564
  97.3 2.4 %copy-start.3 = (bf16[1920,640]{1,0:T(8,128)(2,1)S(1)}, bf16[1920,640]{1,0:T(8,128)(2,1)}, u32[]{:S(2)}) copy-start(bf16[1920,640]{1,0:T(8,128)(2,1)} %get-tuple-element.63) | copy-start | bytes 7372804
  103.9 1.7 copy-start.2
  138.0 11.4 %collective-permute-start.6 = (bf16[640,32,16]{0,2,1:T(8,128)(2,1)S(1)}, bf16[640,32,16]{0,2,1:T(8,128)(2,1)S(1)}, u32[]{:S(2)}, u32[]{:S(2)}) collective-permute-start(bf16[640,32,16]{0,2,1:T(8,128)(2,1)S(1)} %get-tuple-element.59), channel_id=1, source_target_pairs={{0,8},{8,0},{1,9},{9,1},{2,10},{10,2},{3,11},{11,3},{4,12},{12,4},... | collective-permute-start | bytes 1966088 | tf_op jit(solution)/shard_map/ppermute | solution.py:39
  147.2 7.7 %collective-permute-start.5 = (bf16[640,32,80]{0,2,1:T(8,128)(2,1)S(1)}, bf16[640,32,80]{0,2,1:T(8,128)(2,1)S(1)}, u32[]{:S(2)}, u32[]{:S(2)}) collective-permute-start(bf16[640,32,80]{0,2,1:T(8,128)(2,1)S(1)} %slice.211), channel_id=1, source_target_pairs={{0,8},{8,0},{1,9},{9,1},{2,10},{10,2},{3,11},{11,3},{4,12},{12,4},... | collective-permute-start | bytes 9830408 | tf_op jit(solution)/shard_map/ppermute | solution.py:39
Sparse Core Ops, SparseCore 0:
  39.5 42.3 all-gather.1
  162.4 64.0 reduce-scatter.1
